TPU v7x, 32 devices: a whole 2x2x4 slice. The times are simulated.
32 devices in a mesh: dp: 2 (over y), row: 4 (over x, core), col: 4 (over z).
Axes of the slice: x: 2, y: 2, z: 4, core: 2. Of those that a mesh axis runs over, the one named last changes fastest.
Arguments:
- patches: bfloat16 [2, 512, 1456], P('dp', 'col', 'row'), may hold values from -6 to 6
- queries: bfloat16 [2, 512, 6144], P('dp', 'col', 'row'), may hold values from -6 to 6
- attn_keys: bfloat16 [2, 512, 6144], P('dp', 'col', 'row'), may hold values from -6 to 6
- attn_values: bfloat16 [2, 512, 6144], P('dp', 'col', 'row'), may hold values from -6 to 6
- out_weight: bfloat16 [6144, 12288], P('row', 'col'), may hold values from -0.15625 to 0.15625
- output_grad: bfloat16 [2, 512, 12288], P('dp', 'row', 'col'), may hold values from -4 to 4
Outputs:
- query_grad: float32 [2, 512, 6144], P('dp', 'col', 'row')
- key_grad: float32 [2, 512, 6144], P('dp', 'col', 'row')
- value_grad: float32 [2, 512, 6144], P('dp', 'col', 'row')
- out_weight_grad: float32 [6144, 12288], P('row', 'col')
- embed_weight_grad: float32 [1456, 12288], P('row', 'col')
All inputs are finite; a program needn't handle non-finite values.
Results may differ from a plain program's by a relative error of at most 0.025.
Values may be sent and summed in bfloat16 or wider, within the bound.
No kernel may reach another device: no remote copies, remote signals or barrier semaphores. Data moves between devices by JAX's collectives and lax.ppermute only.
A program may use at most 128 MiB of HBM per device.

v0:
```python
import jax
import jax.numpy as jnp
from jax import lax
from jax.sharding import PartitionSpec as P

DH = 128


def contract_rows(left, right):
    return lax.dot_general(
        left, right, (((0,), (0,)), ((), ())), preferred_element_type=jnp.float32
    )


def body(patches, queries, attn_keys, attn_values, out_weight, output_grad):
    factor = DH ** (-0.5)
    local_rows = queries.shape[1]
    feature_width = queries.shape[2]
    head_count = feature_width // DH
    every_key, every_value, every_patch = (
        lax.all_gather(attn_keys, "col", axis=1, tiled=True),
        lax.all_gather(attn_values, "col", axis=1, tiled=True),
        lax.all_gather(patches, "col", axis=1, tiled=True),
    )
    local_query = queries[0].reshape(local_rows, head_count, DH)
    all_keys = every_key[0].reshape(-1, head_count, DH)
    all_values = every_value[0].reshape(-1, head_count, DH)
    scores = (
        jnp.einsum("qhd,khd->hqk", local_query, all_keys, preferred_element_type=jnp.float32)
        * factor
    )
    row_max = jnp.max(scores, axis=2, keepdims=True)
    log_total = row_max + jnp.log(jnp.sum(jnp.exp(scores - row_max), axis=2, keepdims=True))
    attn_probs = jnp.exp(scores - log_total).astype(jnp.bfloat16)
    attn_out = jnp.einsum(
        "hqk,khd->qhd", attn_probs, all_values, preferred_element_type=jnp.float32
    ).astype(jnp.bfloat16)
    out_local = attn_out.reshape(1, local_rows, feature_width)
    dense_grad = lax.all_gather(output_grad, "row", axis=1, tiled=True)[0]
    attn_grad = lax.psum_scatter(
        lax.dot_general(
            dense_grad, out_weight, (((1,), (1,)), ((), ())), preferred_element_type=jnp.float32
        ),
        "col",
        scatter_dimension=0,
        tiled=True,
    ).astype(jnp.bfloat16)
    grad_heads = attn_grad.reshape(local_rows, head_count, DH)
    prob_grad = jnp.einsum(
        "qhd,khd->hqk", grad_heads, all_values, preferred_element_type=jnp.float32
    )
    row_dot = jnp.transpose(
        jnp.sum(grad_heads.astype(jnp.float32) * attn_out.astype(jnp.float32), axis=2)
    )[:, :, None]
    score_grad = (attn_probs.astype(jnp.float32) * (prob_grad - row_dot)).astype(jnp.bfloat16)
    query_grad = (
        jnp.einsum("hqk,khd->qhd", score_grad, all_keys, preferred_element_type=jnp.float32)
        * factor
    )
    every_out = lax.all_gather(out_local, "col", axis=1, tiled=True)
    key_term = (
        jnp.einsum("hqk,qhd->khd", score_grad, local_query, preferred_element_type=jnp.float32)
        * factor
    )
    value_term = jnp.einsum(
        "hqk,qhd->khd", attn_probs, grad_heads, preferred_element_type=jnp.float32
    )
    key_sum, value_sum = (
        lax.psum_scatter(
            key_term.reshape(-1, feature_width).astype(jnp.bfloat16),
            "col",
            scatter_dimension=0,
            tiled=True,
        ).astype(jnp.float32),
        lax.psum_scatter(
            value_term.reshape(-1, feature_width).astype(jnp.bfloat16),
            "col",
            scatter_dimension=0,
            tiled=True,
        ).astype(jnp.float32),
    )
    out_part = contract_rows(every_out[0], dense_grad)
    embed_part = contract_rows(every_patch[0], dense_grad)
    out_weight_grad, embed_weight_grad = (
        lax.psum(out_part.astype(jnp.bfloat16), "dp").astype(jnp.float32),
        lax.psum(embed_part.astype(jnp.bfloat16), "dp").astype(jnp.float32),
    )
    return (
        query_grad.reshape(1, local_rows, feature_width),
        key_sum.reshape(1, local_rows, feature_width),
        value_sum.reshape(1, local_rows, feature_width),
        out_weight_grad,
        embed_weight_grad,
    )


def solution(mesh):
    placed = (
        P("dp", "col", "row"),
        P("dp", "col", "row"),
        P("dp", "col", "row"),
        P("dp", "col", "row"),
        P("row", "col"),
        P("dp", "row", "col"),
    )
    return jax.shard_map(
        body,
        mesh=mesh,
        in_specs=placed,
        out_specs=(
            P("dp", "col", "row"),
            P("dp", "col", "row"),
            P("dp", "col", "row"),
            P("row", "col"),
            P("row", "col"),
        ),
        check_vma=False,
    )
```

profile of v0, /device:TPU:0, one launch (start us, length us, event | category | flops | bytes accessed | tf_op | source)
XLA Modules:
  0.0 593.3 jit_solution(1535676170303104737)
XLA Ops:
  7.9 1.9 copy.22
  9.9 30.9 %all-gather.7.cloned.1.call-done = bf16[1,512,3072]{2,1,0:T(8,128)(2,1)} async-done(((bf16[1,128,3072]{2,1,0:T(8,128)(2,1)}), bf16[1,512,3072]{2,1,0:T(8,128)(2,1)}) %all-gather.7.cloned.1.call-update) | async-done | bytes 3145744 | tf_op jit(solution)/shard_map/all_gather | solution.py:39
  40.8 10.6 %fusion.2 = f32[512,1536]{1,0:T(8,128)} fusion(bf16[1536,3072]{1,0:T(8,128)(2,1)} %param.10, bf16[1,512,3072]{2,1,0:T(8,128)(2,1)} %all-gather.7.cloned.1.call-done), kind=kOutput, calls=%fused_computation.4 | convolution fusion | flops 4831838208 | bytes 15728640 | tf_op jit(solution)/shard_map/dot_general | solution.py:41
  53.7 27.0 %all-gather.5.cloned.1.call-done = bf16[1,512,1536]{1,2,0:T(8,128)(2,1)} async-done(((bf16[1,128,1536]{1,2,0:T(8,128)(2,1)}), bf16[1,512,1536]{1,2,0:T(8,128)(2,1)}) %all-gather.5.cloned.1.call-update) | async-done | bytes 1572880 | tf_op jit(solution)/shard_map/all_gather | solution.py:21
  80.7 2.1 multiply_reduce_fusion
  84.4 57.7 %reduce-scatter.4.cloned.1.call-done = f32[128,1536]{1,0:T(8,128)} async-done(((f32[512,1536]{1,0:T(8,128)}), f32[128,1536]{1,0:T(8,128)}) %reduce-scatter.4.cloned.1.call-update) | async-done | bytes 786448 | tf_op jit(solution)/shard_map/reduce_scatter | solution.py:40
  143.5 38.4 %all-gather.9.cloned.1.call-done = bf16[1,512,1536]{1,2,0:T(8,128)(2,1)} async-done(((bf16[1,128,1536]{1,2,0:T(8,128)(2,1)}), bf16[1,512,1536]{1,2,0:T(8,128)(2,1)}) %all-gather.9.cloned.1.call-update) | async-done | bytes 1572880 | tf_op jit(solution)/shard_map/all_gather | solution.py:22
  181.9 2.7 multiply_reduce_fusion.1
  184.7 2.0 multiply_convert_fusion.1
  186.7 2.7 multiply_convert_fusion
  189.4 2.7 copy.29
  193.8 2.6 copy.30
  196.6 20.1 %all_gather.19 = bf16[1,512,364]{1,2,0:T(8,128)(2,1)S(1)} all-gather(bf16[1,128,364]{1,2,0:T(8,128)(2,1)S(1)} %copy-done.5), channel_id=1, replica_groups=mesh['dp'=2,'row'=4,'col'=4] {'col'}, dimensions={1}, use_global_device_ids=true | all-gather | bytes 465920 | tf_op jit(solution)/shard_map/all_gather | solution.py:23
  216.7 4.6 convolution_convert_fusion.1
  221.3 5.5 all-gather.11.cloned.1.call-done
  226.8 9.3 %convolution_convert_fusion = bf16[1536,3072]{1,0:T(8,128)(2,1)} fusion(bf16[1,512,3072]{2,1,0:T(8,128)(2,1)} %all-gather.7.cloned.1.call-done, bf16[1,512,1536]{1,2,0:T(8,128)(2,1)} %all-gather.11.cloned.1.call-done), kind=kOutput, calls=%fused_computation | convolution fusion | flops 4836556800 | bytes 14155776 | tf_op jit(solution)/shard_map/dot_general | solution.py:10
  238.9 2.3 copy.31
  241.2 21.2 %reduce-scatter.6.cloned.1.call-done = bf16[128,1536]{1,0:T(8,128)(2,1)} async-done(((bf16[512,1536]{1,0:T(8,128)(2,1)}), bf16[128,1536]{1,0:T(8,128)(2,1)}) %reduce-scatter.6.cloned.1.call-update) | async-done | bytes 393232 | tf_op jit(solution)/shard_map/reduce_scatter | solution.py:69
  262.4 2.0 bitcast_convert_fusion.1
  264.4 34.6 %reduce-scatter.8.cloned.1.call-done = bf16[128,1536]{1,0:T(8,128)(2,1)} async-done(((bf16[512,1536]{1,0:T(8,128)(2,1)}), bf16[128,1536]{1,0:T(8,128)(2,1)}) %reduce-scatter.8.cloned.1.call-update) | async-done | bytes 393232 | tf_op jit(solution)/shard_map/reduce_scatter | solution.py:75
  299.0 2.0 bitcast_convert_fusion
  301.0 270.0 %all-reduce.3.cloned.1.call-done = (bf16[1536,3072]{1,0:T(8,128)(2,1)}, bf16[364,3072]{1,0:T(8,128)(2,1)}) async-done(((bf16[1536,3072]{1,0:T(8,128)(2,1)}, bf16[364,3072]{1,0:T(8,128)(2,1)}), (bf16[1536,3072]{1,0:T(8,128)(2,1)}, bf16[364,3072]{1,0:T(8,128)(2,1)})) %all-reduce.3.cloned.1.call-update) | async-done | bytes 11673616 | tf_op jit(solution)/shard_map/psum | solution.py:85
  571.0 12.9 %convert_element_type.71 = f32[1536,3072]{1,0:T(8,128)} convert(bf16[1536,3072]{1,0:T(8,128)(2,1)} %get-tuple-element.15) | non-fusion elementwise | flops 4718592 | bytes 28311552 | tf_op jit(solution)/shard_map/convert_element_type | solution.py:85
  583.8 2.7 convert_element_type.73
  (37 shorter events, 10.7 us)
Async XLA Ops:
  7.2 33.7 %all-gather.7.cloned.1.call-start = ((), (), s32[]{:S(2)}) async-start(), calls=%async_computation.4 | async-start | bytes 3932160 | tf_op jit(solution)/shard_map/all_gather | solution.py:39
  7.9 72.8 %all-gather.5.cloned.1.call-start = ((), (), s32[]{:S(2)}) async-start(), calls=%async_computation.3 | async-start | bytes 1966080 | tf_op jit(solution)/shard_map/all_gather | solution.py:21
  9.9 132.2 %reduce-scatter.4.cloned.1.call-start = ((), (), s32[]{:S(2)}) async-start(), calls=%async_computation.5 | async-start | bytes 3932160 | tf_op jit(solution)/shard_map/reduce_scatter | solution.py:40
  51.4 1.0 copy-start.3
  51.4 2.0 copy-start.4
  51.4 130.4 %all-gather.9.cloned.1.call-start = ((), (), s32[]{:S(2)}) async-start(), calls=%async_computation.6 | async-start | bytes 1966080 | tf_op jit(solution)/shard_map/all_gather | solution.py:22
  53.4 173.4 %all-gather.11.cloned.1.call-start = ((), (), s32[]{:S(2)}) async-start(), calls=%async_computation.9 | async-start | bytes 1966080 | tf_op jit(solution)/shard_map/all_gather | solution.py:60
  53.6 30.2 %copy-start.1 = (bf16[1,128,1536]{1,2,0:T(8,128)(2,1)}, bf16[1,128,1536]{1,2,0:T(8,128)(2,1)S(1)}, u32[]{:S(2)}) copy-start(bf16[1,128,1536]{1,2,0:T(8,128)(2,1)S(1)} %copy.21) | copy-start | bytes 1179652
  184.6 77.8 %reduce-scatter.6.cloned.1.call-start = ((), (), s32[]{:S(2)}) async-start(), calls=%async_computation.7 | async-start | bytes 1966080 | tf_op jit(solution)/shard_map/reduce_scatter | solution.py:69
  192.1 106.9 %reduce-scatter.8.cloned.1.call-start = ((), (), s32[]{:S(2)}) async-start(), calls=%async_computation.8 | async-start | bytes 1966080 | tf_op jit(solution)/shard_map/reduce_scatter | solution.py:75
  193.8 2.7 copy-start.5
  196.5 374.5 %all-reduce.3.cloned.1.call-start = ((), (), s32[]{:S(2)}) async-start(), calls=%async_computation.10 | async-start | bytes 23396352 | tf_op jit(solution)/shard_map/psum | solution.py:85
  236.1 1.4 copy-start
  571.0 12.9 %copy-start.2 = (bf16[364,3072]{1,0:T(8,128)(2,1)S(1)}, bf16[364,3072]{1,0:T(8,128)(2,1)}, u32[]{:S(2)}) copy-start(bf16[364,3072]{1,0:T(8,128)(2,1)} %get-tuple-element.16) | copy-start | bytes 6709252
Sparse Core Ops, SparseCore 0:
  9.6 31.2 all-gather.6
  43.0 37.7 all-gather.4
  83.6 58.4 reduce-scatter.3
  144.1 37.7 all-gather.8
  184.7 41.9 all-gather.10
  228.9 33.4 reduce-scatter.5
  264.7 34.2 reduce-scatter.7
  302.1 268.8 all-reduce.2
where the time goes:
time: 594 us; the launch traced here: 593 us
  waiting for transfers between devices  486 us (82%)
  matrix products  37.2 us (6%)
  other arithmetic  22.1 us (4%)
  blocking collectives  20.1 us (3%)
  between operations  14.2 us (2%)
  local copies, waits for them, and re-layouts  13.2 us (2%)
    psum x1, waiting for transfers between devices, body(): lax.psum(out_part.astype(jnp.bfloat16), 'dp').astype(jnp.float32)  270 us
    reduce_scatter x1, waiting for transfers between devices, body(): lax.psum_scatter(lax.dot_general(dense_grad, out_weight, (((1,), (1,)), (...  57.7 us
    all_gather x1, waiting for transfers between devices, body(): lax.all_gather(attn_values, 'col', axis=1, tiled=True)  38.4 us
    reduce_scatter x1, waiting for transfers between devices, body(): lax.psum_scatter(value_term.reshape(-1, feature_width).astype(jnp.bfloat1...  34.6 us
    all_gather x1, waiting for transfers between devices, body(): dense_grad = lax.all_gather(output_grad, 'row', axis=1, tiled=True)[0]  30.9 us
    all_gather x1, waiting for transfers between devices, body(): lax.all_gather(attn_keys, 'col', axis=1, tiled=True)  27 us
    reduce_scatter x1, waiting for transfers between devices, body(): lax.psum_scatter(key_term.reshape(-1, feature_width).astype(jnp.bfloat16)...  21.2 us
    all_gather x1, blocking collectives, body(): lax.all_gather(patches, 'col', axis=1, tiled=True)  20.1 us
  transfers between devices with their start and end apart: 8, of which 8 were waited for; matrix products, arithmetic and copies ran while one was open for 9% of the time, Pallas kernels for 0%

commit v1 on v0

--- a/solution.py
+++ b/solution.py
@@ -82,7 +82,7 @@
     out_part = contract_rows(every_out[0], dense_grad)
     embed_part = contract_rows(every_patch[0], dense_grad)
     out_weight_grad, embed_weight_grad = (
-        lax.psum(out_part.astype(jnp.bfloat16), "dp").astype(jnp.float32),
+        jnp.sum(lax.all_gather(out_part.astype(jnp.bfloat16), "dp"), axis=0).astype(jnp.float32),
         lax.psum(embed_part.astype(jnp.bfloat16), "dp").astype(jnp.float32),
     )
     return (

time: 594 us -> 628 us (1.057)
  waiting for transfers between devices: 486 us -> 507 us
  other arithmetic: 22.1 us -> 40.5 us
    all_gather x0 -> x1, waiting for transfers between devices: none -> 224 us  [body(): lax.all_gather(out_part.astype(jnp.bfloat16), 'dp')]
    psum x1, waiting for transfers between devices: 270 us -> 60.1 us  [body(): lax.psum(embed_part.astype(jnp.bfloat16), 'dp').astype(jnp.float32)]
    reduce_sum x0 -> x1, other arithmetic: none -> 16.8 us  [body(): jnp.sum(lax.all_gather(out_part.astype(jnp.bfloat16), 'dp'), axis=0)]
    reduce_scatter x1, waiting for transfers between devices: 21.2 us -> 29.6 us  [body(): lax.psum_scatter(key_term.reshape(-1, feature_width).astype(jnp.bfloat16)...]
  transfers between devices with their start and end apart: 8 -> 9, of which waited for: 8 -> 9; matrix products, arithmetic and copies ran while one was open for 9% -> 9% of each run, Pallas kernels for 0% -> 0%
where the time goes in v1:
time: 628 us; the launch traced here: 627 us
  waiting for transfers between devices  507 us (81%)
  other arithmetic  40.5 us (6%)
  matrix products  37.4 us (6%)
  blocking collectives  16.3 us (3%)
  between operations  13.9 us (2%)
  local copies, waits for them, and re-layouts  11.8 us (2%)
    all_gather x1, waiting for transfers between devices, body(): lax.all_gather(out_part.astype(jnp.bfloat16), 'dp')  224 us
    psum x1, waiting for transfers between devices, body(): lax.psum(embed_part.astype(jnp.bfloat16), 'dp').astype(jnp.float32)  60.1 us
    reduce_scatter x1, waiting for transfers between devices, body(): lax.psum_scatter(lax.dot_general(dense_grad, out_weight, (((1,), (1,)), (...  57.7 us
    all_gather x1, waiting for transfers between devices, body(): lax.all_gather(attn_values, 'col', axis=1, tiled=True)  38.4 us
    reduce_scatter x1, waiting for transfers between devices, body(): lax.psum_scatter(value_term.reshape(-1, feature_width).astype(jnp.bfloat1...  34.7 us
    all_gather x1, waiting for transfers between devices, body(): dense_grad = lax.all_gather(output_grad, 'row', axis=1, tiled=True)[0]  30.9 us
    reduce_scatter x1, waiting for transfers between devices, body(): lax.psum_scatter(key_term.reshape(-1, feature_width).astype(jnp.bfloat16)...  29.6 us
    all_gather x1, waiting for transfers between devices, body(): lax.all_gather(attn_keys, 'col', axis=1, tiled=True)  27 us
  transfers between devices with their start and end apart: 9, of which 9 were waited for; matrix products, arithmetic and copies ran while one was open for 9% of the time, Pallas kernels for 0%

profile of v1, /device:TPU:0, one launch (start us, length us, event | category | flops | bytes accessed | tf_op | source)
XLA Modules:
  0.0 627.1 jit_solution(8002021358424501275)
XLA Ops:
  9.9 30.9 %all-gather.9.cloned.1.call-done = bf16[1,512,3072]{2,1,0:T(8,128)(2,1)} async-done(((bf16[1,128,3072]{2,1,0:T(8,128)(2,1)}), bf16[1,512,3072]{2,1,0:T(8,128)(2,1)}) %all-gather.9.cloned.1.call-update) | async-done | bytes 3145744 | tf_op jit(solution)/shard_map/all_gather | solution.py:39
  40.8 10.6 %fusion.2 = f32[512,1536]{1,0:T(8,128)} fusion(bf16[1536,3072]{1,0:T(8,128)(2,1)} %param.10, bf16[1,512,3072]{2,1,0:T(8,128)(2,1)} %all-gather.9.cloned.1.call-done), kind=kOutput, calls=%fused_computation.4 | convolution fusion | flops 4831838208 | bytes 15728640 | tf_op jit(solution)/shard_map/dot_general | solution.py:41
  53.7 27.0 %all-gather.7.cloned.1.call-done = bf16[1,512,1536]{1,2,0:T(8,128)(2,1)} async-done(((bf16[1,128,1536]{1,2,0:T(8,128)(2,1)}), bf16[1,512,1536]{1,2,0:T(8,128)(2,1)}) %all-gather.7.cloned.1.call-update) | async-done | bytes 1572880 | tf_op jit(solution)/shard_map/all_gather | solution.py:21
  80.7 2.1 multiply_reduce_fusion
  84.4 57.7 %reduce-scatter.4.cloned.1.call-done = f32[128,1536]{1,0:T(8,128)} async-done(((f32[512,1536]{1,0:T(8,128)}), f32[128,1536]{1,0:T(8,128)}) %reduce-scatter.4.cloned.1.call-update) | async-done | bytes 786448 | tf_op jit(solution)/shard_map/reduce_scatter | solution.py:40
  143.5 38.4 %all-gather.11.cloned.1.call-done = bf16[1,512,1536]{1,2,0:T(8,128)(2,1)} async-done(((bf16[1,128,1536]{1,2,0:T(8,128)(2,1)}), bf16[1,512,1536]{1,2,0:T(8,128)(2,1)}) %all-gather.11.cloned.1.call-update) | async-done | bytes 1572880 | tf_op jit(solution)/shard_map/all_gather | solution.py:22
  181.9 2.7 multiply_reduce_fusion.1
  184.7 16.3 %all_gather.27 = bf16[1,512,364]{1,2,0:T(8,128)(2,1)S(1)} all-gather(bf16[1,128,364]{1,2,0:T(8,128)(2,1)S(1)} %copy-done.4), channel_id=1, replica_groups=mesh['dp'=2,'row'=4,'col'=4] {'col'}, dimensions={1}, use_global_device_ids=true | all-gather | bytes 465920 | tf_op jit(solution)/shard_map/all_gather | solution.py:23
  200.9 4.6 convolution_convert_fusion.1
  205.7 2.1 multiply_convert_fusion.1
  207.7 2.7 multiply_convert_fusion
  210.4 2.6 copy.29
  214.8 2.7 copy.30
  217.7 4.0 all-gather.13.cloned.1.call-done
  221.7 9.5 %convolution_convert_fusion = bf16[1536,3072]{1,0:T(8,128)(2,1)} fusion(bf16[1,512,3072]{2,1,0:T(8,128)(2,1)} %all-gather.9.cloned.1.call-done, bf16[1,512,1536]{1,2,0:T(8,128)(2,1)} %all-gather.13.cloned.1.call-done), kind=kOutput, calls=%fused_computation | convolution fusion | flops 4836556800 | bytes 14155776 | tf_op jit(solution)/shard_map/dot_general | solution.py:10
  231.2 60.1 %all-reduce.2.cloned.1.call-done = bf16[364,3072]{1,0:T(8,128)(2,1)} async-done(((bf16[364,3072]{1,0:T(8,128)(2,1)}), bf16[364,3072]{1,0:T(8,128)(2,1)}) %all-reduce.2.cloned.1.call-update) | async-done | bytes 2236432 | tf_op jit(solution)/shard_map/psum | solution.py:86
  291.3 4.3 convert_element_type.75
  297.1 2.3 copy.31
  299.4 29.6 %reduce-scatter.6.cloned.1.call-done = bf16[128,1536]{1,0:T(8,128)(2,1)} async-done(((bf16[512,1536]{1,0:T(8,128)(2,1)}), bf16[128,1536]{1,0:T(8,128)(2,1)}) %reduce-scatter.6.cloned.1.call-update) | async-done | bytes 393232 | tf_op jit(solution)/shard_map/reduce_scatter | solution.py:69
  328.9 2.0 bitcast_convert_fusion.1
  330.9 34.7 %reduce-scatter.8.cloned.1.call-done = bf16[128,1536]{1,0:T(8,128)(2,1)} async-done(((bf16[512,1536]{1,0:T(8,128)(2,1)}), bf16[128,1536]{1,0:T(8,128)(2,1)}) %reduce-scatter.8.cloned.1.call-update) | async-done | bytes 393232 | tf_op jit(solution)/shard_map/reduce_scatter | solution.py:75
  367.5 223.5 %all-gather.15.cloned.1.call-done = bf16[3072,3072]{1,0:T(8,128)(2,1)} async-done(((bf16[1536,3072]{1,0:T(8,128)(2,1)}), bf16[3072,3072]{1,0:T(8,128)(2,1)}) %all-gather.15.cloned.1.call-update) | async-done | bytes 18874384 | tf_op jit(solution)/shard_map/all_gather | solution.py:85
  591.1 16.8 %reduce_sum.32 = bf16[1536,3072]{1,0:T(8,128)(2,1)} reduce(bf16[2,1536,3072]{2,1,0:T(8,128)(2,1)} %bitcast.51, bf16[]{:T(256)} %constant.3.clone.1), dimensions={0}, to_apply=%region_6.0 | reduce | flops 4718592 | bytes 28311554 | tf_op jit(solution)/shard_map/reduce_sum | solution.py:85
  607.9 12.8 %convert_element_type.73 = f32[1536,3072]{1,0:T(8,128)} convert(bf16[1536,3072]{1,0:T(8,128)(2,1)} %reduce_sum.32) | non-fusion elementwise | flops 4718592 | bytes 28311552 | tf_op jit(solution)/shard_map/convert_element_type | solution.py:85
  (39 shorter events, 13.4 us)
Async XLA Ops:
  7.2 33.7 %all-gather.9.cloned.1.call-start = ((), (), s32[]{:S(2)}) async-start(), calls=%async_computation.4 | async-start | bytes 3932160 | tf_op jit(solution)/shard_map/all_gather | solution.py:39
  7.9 72.8 %all-gather.7.cloned.1.call-start = ((), (), s32[]{:S(2)}) async-start(), calls=%async_computation.3 | async-start | bytes 1966080 | tf_op jit(solution)/shard_map/all_gather | solution.py:21
  9.9 132.2 %reduce-scatter.4.cloned.1.call-start = ((), (), s32[]{:S(2)}) async-start(), calls=%async_computation.5 | async-start | bytes 3932160 | tf_op jit(solution)/shard_map/reduce_scatter | solution.py:40
  51.4 1.0 copy-start.2
  51.4 2.0 copy-start.3
  51.4 130.4 %all-gather.11.cloned.1.call-start = ((), (), s32[]{:S(2)}) async-start(), calls=%async_computation.6 | async-start | bytes 1966080 | tf_op jit(solution)/shard_map/all_gather | solution.py:22
  53.4 168.4 %all-gather.13.cloned.1.call-start = ((), (), s32[]{:S(2)}) async-start(), calls=%async_computation.9 | async-start | bytes 1966080 | tf_op jit(solution)/shard_map/all_gather | solution.py:60
  53.6 30.2 %copy-start.1 = (bf16[1,128,1536]{1,2,0:T(8,128)(2,1)}, bf16[1,128,1536]{1,2,0:T(8,128)(2,1)S(1)}, u32[]{:S(2)}) copy-start(bf16[1,128,1536]{1,2,0:T(8,128)(2,1)S(1)} %copy.21) | copy-start | bytes 1179652
  84.4 100.3 %copy-start.4 = (bf16[1,128,364]{1,2,0:T(8,128)(2,1)S(1)}, bf16[1,128,364]{1,2,0:T(8,128)(2,1)}, u32[]{:S(2)}) copy-start(bf16[1,128,364]{1,2,0:T(8,128)(2,1)} %param.6) | copy-start | bytes 279556
  184.6 106.7 %all-reduce.2.cloned.1.call-start = ((), (), s32[]{:S(2)}) async-start(), calls=%async_computation.10 | async-start | bytes 4521984 | tf_op jit(solution)/shard_map/psum | solution.py:86
  205.6 123.3 %reduce-scatter.6.cloned.1.call-start = ((), (), s32[]{:S(2)}) async-start(), calls=%async_computation.7 | async-start | bytes 1966080 | tf_op jit(solution)/shard_map/reduce_scatter | solution.py:69
  213.0 152.5 %reduce-scatter.8.cloned.1.call-start = ((), (), s32[]{:S(2)}) async-start(), calls=%async_computation.8 | async-start | bytes 1966080 | tf_op jit(solution)/shard_map/reduce_scatter | solution.py:75
  217.5 373.6 %all-gather.15.cloned.1.call-start = ((), (), s32[]{:S(2)}) async-start(), calls=%async_computation.11 | async-start | bytes 28311552 | tf_op jit(solution)/shard_map/all_gather | solution.py:85
  231.2 64.4 %copy-start = (bf16[1,512,1536]{1,2,0:T(8,128)(2,1)S(1)}, bf16[1,512,1536]{1,2,0:T(8,128)(2,1)}, u32[]{:S(2)}) copy-start(bf16[1,512,1536]{1,2,0:T(8,128)(2,1)} %all-gather.7.cloned.1.call-done) | copy-start | bytes 4718596
Sparse Core Ops, SparseCore 0:
  9.6 31.2 all-gather.8
  43.0 37.7 all-gather.6
  83.6 58.4 reduce-scatter.3
  144.1 37.7 all-gather.10
  184.7 36.9 all-gather.12
  224.4 66.8 all-reduce.1
  293.6 35.2 reduce-scatter.5
  331.2 34.2 reduce-scatter.7
  367.7 223.3 all-gather.14
